TPU v7x, 32 devices: a whole 2x2x4 slice. The times are simulated.
32 devices in a mesh: row: 8 (over z, y), col: 4 (over x, core).
Axes of the slice: x: 2, y: 2, z: 4, core: 2. Of those that a mesh axis runs over, the one named last changes fastest.
Arguments:
- density: float32 [4, 256, 2048], P('col', 'row'), may hold values from 0.5 to 2
- momentum: float32 [3, 4, 256, 2048], P(None, 'col', 'row'), may hold values from -6 to 6
- energy: float32 [4, 256, 2048], P('col', 'row'), may hold values from 2 to 5
Outputs:
- tendency: float32 [5, 4, 256, 2048], P(None, 'col', 'row')
All inputs are finite; a program needn't handle non-finite values.
Results may differ from a plain program's by a relative error of at most 0.000053.
Values sent between devices are 32-bit elements; how exact they have to be, the bound alone decides.
No kernel may reach another device: no remote copies, remote signals or barrier semaphores. Data moves between devices by JAX's collectives and lax.ppermute only.
A program may use at most 64 MiB of HBM per device.

v0:
```python
import jax
import jax.numpy as jnp
import numpy as np
from jax import lax
from jax.sharding import PartitionSpec as P


def operator_column(count):
    steps = np.arange(count)
    wave = 2.0 * np.pi * steps / count
    upper = (
        17.0 / 12.0 * np.sin(wave)
        + 101.0 / 300.0 * np.sin(2.0 * wave)
        + 1.0 / 300.0 * np.sin(3.0 * wave)
    )
    lower = 1.0 + np.cos(wave) + 0.1 * np.cos(2.0 * wave)
    ratio = upper / lower
    phase = 2.0 * np.pi * (steps[:, None] * steps[None, :] % count) / count
    return -np.sum(ratio[:, None] * np.sin(phase), axis=0) / count


def operator_table(count):
    column = operator_column(count)
    steps = np.arange(count)
    offsets = (steps[None, :] - steps[:, None]) % count
    return column[offsets].astype(np.float32)


def block_weights(count):
    table = operator_table(count)
    width = 128
    w_self = table[:width, :width]
    w_prev = table[:width, width : 2 * width]
    w_next = table[width : 2 * width, :width]
    return jnp.asarray(np.concatenate([w_prev, w_self, w_next], axis=1))


def compact_last(field):
    count = field.shape[-1]
    width = 128
    blocks = field.reshape(field.shape[:-1] + (count // width, width))
    parts = jnp.einsum(
        "...bj,jk->...bk", blocks, block_weights(count), precision=lax.Precision.HIGHEST
    )
    result = (
        jnp.roll(parts[..., :width], 1, axis=-2)
        + parts[..., width : 2 * width]
        + jnp.roll(parts[..., 2 * width :], -1, axis=-2)
    )
    return result.reshape(field.shape)


def compact_second(field):
    count = field.shape[-2]
    if count <= 256:
        weights = jnp.asarray(operator_table(count))
        return jnp.einsum("...jc,ji->...ic", field, weights, precision=lax.Precision.HIGHEST)
    width = 128
    blocks = field.reshape(field.shape[:-2] + (count // width, width, field.shape[-1]))
    parts = jnp.einsum(
        "...bjc,jk->...bkc", blocks, block_weights(count), precision=lax.Precision.HIGHEST
    )
    result = (
        jnp.roll(parts[..., :width, :], 1, axis=-3)
        + parts[..., width : 2 * width, :]
        + jnp.roll(parts[..., 2 * width :, :], -1, axis=-3)
    )
    return result.reshape(field.shape)


def fluxes(density, momentum, energy):
    speed = momentum / density[None]
    pressure = 0.4 * (energy - 0.5 * jnp.sum(momentum * momentum, axis=0) / density)
    enthalpy = energy + pressure
    vel_x, vel_y = (speed[0], speed[1])
    flux_x = jnp.stack(
        [
            momentum[0],
            momentum[0] * vel_x + pressure,
            momentum[1] * vel_x,
            momentum[2] * vel_x,
            enthalpy * vel_x,
        ]
    )
    flux_y = jnp.stack(
        [
            momentum[1],
            momentum[0] * vel_y,
            momentum[1] * vel_y + pressure,
            momentum[2] * vel_y,
            enthalpy * vel_y,
        ],
        axis=2,
    )
    return (flux_x, flux_y)


def local(density, momentum, energy):
    flux_x, flux_y = fluxes(density, momentum, energy)
    planes, owned, length = (flux_y.shape[0], flux_y.shape[1], flux_y.shape[3])
    packed = flux_y.reshape(planes, owned, 5 * length)
    derivative_x = compact_last(flux_x)
    y_lines = lax.all_to_all(packed, "row", split_axis=2, concat_axis=1, tiled=True)
    derivative_lines = compact_second(y_lines)
    derived = lax.all_to_all(derivative_lines, "row", split_axis=1, concat_axis=2, tiled=True)
    derivative_y = jnp.transpose(derived.reshape(planes, owned, 5, length), (2, 0, 1, 3))
    return -(derivative_x + derivative_y)


def solution(mesh):
    in_specs = (P("col", "row", None), P(None, "col", "row", None), P("col", "row", None))
    out_specs = P(None, "col", "row", None)
    return jax.shard_map(local, mesh=mesh, in_specs=in_specs, out_specs=out_specs, check_vma=False)
```

profile of v0, /device:TPU:0, one launch (start us, length us, event | category | flops | bytes accessed | tf_op | source)
XLA Modules:
  0.0 174.0 jit_solution(4821467168655819884)
XLA Ops:
  0.0 1.0 bitcast_dynamic-update-slice_fusion.9
  1.0 0.0 copy-start.1
  1.1 0.0 copy-start.2
  1.1 1.4 multiply_reduce_fusion
  2.5 0.0 copy-done
  2.5 0.0 copy-done.1
  2.5 0.1 bitcast_dynamic-update-slice_fusion.7
  2.7 3.8 %copy.31 = f32[1,32,5,2048]{1,3,2,0:T(8,128)} copy(f32[1,32,5,2048]{3,1,2,0:T(8,128)S(1)} %bitcast_dynamic-update-slice_fusion.5) | data formatting | bytes 2621440 | tf_op jit(solution)/shard_map/reshape | solution.py:101
  6.5 0.5 broadcast.11
  7.0 47.4 %reduce.1 = f32[10240,32]{1,0:T(8,128)} reduce(f32[10240,1,32]{2,1,0:T(1,128)} %bitcast.106, f32[]{:T(128)} %broadcast.11), dimensions={1}, to_apply=%bitcast.93.reduce_sub_computation | reduce | bytes 2621444
  54.4 5.3 %reshape.146 = f32[8,1,40960]{2,1,0:T(1,128)} reshape(f32[10240,32]{1,0:T(8,128)} %reduce.1) | data formatting | bytes 2621440
  59.8 38.7 %all_to_all.30 = f32[8,1,40960]{2,1,0:T(1,128)S(1)} all-to-all(f32[8,1,40960]{2,1,0:T(1,128)} %reshape.146), channel_id=1, replica_groups=mesh['row'=8,'col'=4] {'row'}, dimensions={0} | all-to-all | bytes 2621440 | tf_op jit(solution)/shard_map/all_to_all | solution.py:103
  98.4 5.2 %reduce.2 = f32[8,40960]{1,0:T(8,128)} reduce(f32[8,1,40960]{2,1,0:T(1,128)S(1)} %all_to_all.30, f32[]{:T(128)} %broadcast.11), dimensions={1}, to_apply=%all_to_all.22.reduce_sub_computation | reduce | bytes 2621444 | tf_op jit(solution)/shard_map/all_to_all | solution.py:103
  103.7 12.0 %reshape.147 = f32[10240,1,32]{2,1,0:T(1,128)} reshape(f32[8,40960]{1,0:T(8,128)} %reduce.2) | data formatting | bytes 2621440
  115.6 10.6 %copy.26 = f32[1,32,10240]{2,1,0:T(8,128)} copy(f32[1,32,10240]{1,0,2:T(1,128)} %bitcast.107) | data formatting | bytes 2621440 | tf_op jit(solution)/shard_map/all_to_all | solution.py:103
  126.2 1.5 reshape.141
  127.8 2.2 %convolution_bitcast_fusion = f32[1,256,1280]{2,1,0:T(8,128)S(1)} fusion(f32[256,256]{1,0:T(8,128)} %constant.17, f32[256,1280]{1,0:T(8,128)S(1)} %reshape.141), kind=kOutput, calls=%fused_computation | convolution fusion | flops 1006632960 | bytes 2883584 | tf_op jit(solution)/shard_map/...jc,ji->...ic/dot_general | solution.py:57
  130.0 2.4 %copy.27 = f32[1,256,1280]{2,0,1:T(1,128)} copy(f32[1,256,1280]{2,1,0:T(8,128)S(1)} %convolution_bitcast_fusion) | data formatting | bytes 2621440 | tf_op jit(solution)/shard_map/...jc,ji->...ic/transpose | solution.py:57
  132.4 4.3 %all-to-all-start.1 = ((f32[1,256,1280]{2,0,1:T(1,128)}), f32[1,256,1280]{2,0,1:T(1,128)}, u32[]{:S(2)}, u32[]{:S(2)}) async-start(f32[1,256,1280]{2,0,1:T(1,128)} %copy.27), calls=%async_computation.1 | async-start | bytes 2621440 | tf_op jit(solution)/shard_map/all_to_all | solution.py:105
  136.6 0.1 multiply_bitcast_fusion
  136.9 0.1 fusion.7
  137.1 0.0 copy-start.3
  137.2 0.8 copy-done.3
  138.0 3.5 %convolution_bitcast_fusion.1 = f32[5,1,32,16,384]{4,3,2,0,1:T(8,128)S(1)} fusion(f32[5,32,16,128]{3,2,1,0:T(8,128)S(1)} %bitcast_dynamic-update-slice_fusion, f32[128,384,1,1]{1,0,3,2:T(8,128)S(1)} %copy-done.3), kind=kOutput, calls=%fused_computation.1 | convolution fusion | flops 1509949440 | bytes 5439488 | tf_op jit(solution)/shard_map/...bj,jk->...bk/dot_general | solution.py:42
  141.5 0.1 fusion.10
  141.6 0.2 fusion.9
  141.9 0.4 fusion
  142.2 0.2 reshape.137
  142.4 24.9 %all-to-all-done.1 = f32[1,256,1280]{2,0,1:T(1,128)} async-done(((f32[1,256,1280]{2,0,1:T(1,128)}), f32[1,256,1280]{2,0,1:T(1,128)}, u32[]{:S(2)}, u32[]{:S(2)}) %all-to-all-start.1) | async-done | bytes 1310752 | tf_op jit(solution)/shard_map/all_to_all | solution.py:105
  167.3 3.1 %copy.40 = f32[1,8,32,1280]{3,1,2,0:T(8,128)} copy(f32[1,8,32,1280]{3,0,2,1:T(1,128)} %bitcast.16) | data formatting | bytes 2621440 | tf_op jit(solution)/shard_map/all_to_all | solution.py:105
  170.5 1.5 reshape.140
  172.0 2.0 %fusion.1 = f32[5,1,32,2048]{3,2,1,0:T(8,128)} fusion(f32[5,1,32,2048]{3,2,1,0:T(8,128)S(1)} %reshape.137, f32[1,32,5,2048]{3,2,1,0:T(8,128)S(1)} %reshape.140), kind=kLoop, calls=%fused_computation.5 | loop fusion | flops 655360 | bytes 3932160 | tf_op jit(solution)/shard_map/neg | solution.py:107
  (15 shorter events, 0.5 us)
Async XLA Ops:
  0.0 2.5 %copy-start = (f32[3,1,32,2048]{3,2,1,0:T(8,128)S(1)}, f32[3,1,32,2048]{3,2,1,0:T(8,128)}, u32[]{:S(2)}) copy-start(f32[3,1,32,2048]{3,2,1,0:T(8,128)} %param.6) | copy-start | bytes 2359300
  1.0 1.5 copy-start.1
  1.1 1.5 copy-start.2
  132.4 35.0 %all-to-all-start.1 = ((f32[1,256,1280]{2,0,1:T(1,128)}), f32[1,256,1280]{2,0,1:T(1,128)}, u32[]{:S(2)}, u32[]{:S(2)}) async-start(f32[1,256,1280]{2,0,1:T(1,128)} %copy.27), calls=%async_computation.1 | async-start | bytes 2621440 | tf_op jit(solution)/shard_map/all_to_all | solution.py:105
  137.1 0.9 copy-start.3
where the time goes:
time: 175 us; the launch traced here: 174 us
  other arithmetic  56.7 us (32%)
  local copies, waits for them, and re-layouts  43.5 us (25%)
  blocking collectives  38.7 us (22%)
  waiting for transfers between devices  24.9 us (14%)
  matrix products  5.71 us (3%)
  starting transfers between devices  4.26 us (2%)
    unnamed x6, other arithmetic  47.7 us
    all_to_all x1, blocking collectives, local(): lax.all_to_all(packed, 'row', split_axis=2, concat_axis=1, tiled=True)  38.7 us
    all_to_all x1, waiting for transfers between devices, local(): lax.all_to_all(derivative_lines, 'row', split_axis=1, concat_axis=2, tile...  24.9 us
    unnamed x21, local copies, waits for them, and re-layouts  20 us
    all_to_all x1, local copies, waits for them, and re-layouts, local(): lax.all_to_all(packed, 'row', split_axis=2, concat_axis=1, tiled=True)  10.6 us
    all_to_all x1, other arithmetic, local(): lax.all_to_all(packed, 'row', split_axis=2, concat_axis=1, tiled=True)  5.24 us
    all_to_all x1, starting transfers between devices, local(): lax.all_to_all(derivative_lines, 'row', split_axis=1, concat_axis=2, tile...  4.26 us
    reshape x1, local copies, waits for them, and re-layouts, local(): packed = flux_y.reshape(planes, owned, 5 * length)  3.76 us
  transfers between devices with their start and end apart: 1, of which 1 were waited for; matrix products, arithmetic and copies ran while one was open for 3% of the time, Pallas kernels for 0%

commit v1 on v0

--- a/solution.py
+++ b/solution.py
@@ -100,7 +100,10 @@
     planes, owned, length = (flux_y.shape[0], flux_y.shape[1], flux_y.shape[3])
     packed = flux_y.reshape(planes, owned, 5 * length)
     derivative_x = compact_last(flux_x)
-    y_lines = lax.all_to_all(packed, "row", split_axis=2, concat_axis=1, tiled=True)
+    y_lines = jnp.concatenate(
+        lax.all_to_all(jnp.stack(jnp.split(packed, lax.axis_size("row"), axis=2)), "row", 0, 0),
+        axis=1,
+    )
     derivative_lines = compact_second(y_lines)
     derived = lax.all_to_all(derivative_lines, "row", split_axis=1, concat_axis=2, tiled=True)
     derivative_y = jnp.transpose(derived.reshape(planes, owned, 5, length), (2, 0, 1, 3))

time: 175 us -> 87.2 us (0.50)
  other arithmetic: 56.7 us -> 3.99 us
  local copies, waits for them, and re-layouts: 43.5 us -> 10 us
    unnamed x6 -> x5, other arithmetic: 47.7 us -> 0.26 us
    unnamed x21 -> x27, local copies, waits for them, and re-layouts: 20 us -> 2.27 us
    all_to_all x1 -> x0, local copies, waits for them, and re-layouts: 10.6 us -> none  [local(): lax.all_to_all(packed, 'row', split_axis=2, concat_axis=1, tiled=True)]
    all_to_all x1 -> x0, other arithmetic: 5.24 us -> none  [local(): lax.all_to_all(packed, 'row', split_axis=2, concat_axis=1, tiled=True)]
    reshape x1, local copies, waits for them, and re-layouts: 3.76 us -> 0.11 us  [local(): packed = flux_y.reshape(planes, owned, 5 * length)]
  transfers between devices with their start and end apart: 1 -> 1, of which waited for: 1 -> 1; matrix products, arithmetic and copies ran while one was open for 3% -> 6% of each run, Pallas kernels for 0% -> 0%
where the time goes in v1:
time: 87.2 us; the launch traced here: 86.9 us
  blocking collectives  38.6 us (44%)
  waiting for transfers between devices  24.9 us (29%)
  local copies, waits for them, and re-layouts  10 us (11%)
  matrix products  4.77 us (5%)
  starting transfers between devices  4.26 us (5%)
  other arithmetic  3.99 us (5%)
    all_to_all x1, blocking collectives, local(): lax.all_to_all(jnp.stack(jnp.split(packed, lax.axis_size('row'), axis=2))...  38.6 us
    all_to_all x1, waiting for transfers between devices, local(): lax.all_to_all(derivative_lines, 'row', split_axis=1, concat_axis=2, tile...  24.9 us
    all_to_all x1, starting transfers between devices, local(): lax.all_to_all(derivative_lines, 'row', split_axis=1, concat_axis=2, tile...  4.26 us
    dot_general x1, matrix products, compact_last(): jnp.einsum('...bj,jk->...bk', blocks, block_weights(count), precision=lax...  3.51 us
    all_to_all x1, local copies, waits for them, and re-layouts, local(): lax.all_to_all(derivative_lines, 'row', split_axis=1, concat_axis=2, tile...  3.13 us
    transpose x1, local copies, waits for them, and re-layouts, compact_second(): jnp.einsum('...jc,ji->...ic', field, weights, precision=lax.Precision.HIG...  2.4 us
    unnamed x27, local copies, waits for them, and re-layouts  2.27 us
    neg x1, other arithmetic, local(): return -(derivative_x + derivative_y)  1.96 us
  transfers between devices with their start and end apart: 1, of which 1 were waited for; matrix products, arithmetic and copies ran while one was open for 6% of the time, Pallas kernels for 0%

profile of v1, /device:TPU:0, one launch (start us, length us, event | category | flops | bytes accessed | tf_op | source)
XLA Modules:
  0.0 86.9 jit_solution(5727893752712151912)
XLA Ops:
  0.0 0.0 copy-start
  0.0 1.0 %bitcast_dynamic-update-slice_fusion.9 = f32[1,32,5,2048]{3,1,2,0:T(8,128)S(1)} fusion(f32[3,1,32,2048]{3,2,1,0:T(8,128)} %param.6), kind=kLoop, calls=%fused_computation.21 | loop fusion | bytes 524288
  1.0 0.0 copy-start.1
  1.1 0.0 copy-start.2
  1.1 1.4 %multiply_reduce_fusion = (f32[32,2048]{1,0:T(8,128)S(1)}, f32[3,1,32,2048]{3,2,1,0:T(8,128)S(1)}) fusion(f32[3,1,32,2048]{3,2,1,0:T(8,128)} %param.6, f32[32,2048]{1,0:T(8,128)} %bitcast.154), kind=kLoop, calls=%fused_computation.7 | loop fusion | flops 524288 | bytes 2097152 | tf_op jit(solution)/shard_map/reduce_sum | solution.py:73
  2.5 0.0 copy-done
  2.5 0.0 copy-done.1
  2.5 0.0 copy-done.2
  2.5 0.1 bitcast_dynamic-update-slice_fusion.7
  2.7 0.1 copy.21
  3.0 0.0 copy-start.3
  3.0 38.6 %all_to_all.20 = f32[8,1,32,1280]{3,2,1,0:T(8,128)S(1)} all-to-all(f32[8,1,32,1280]{3,2,1,0:T(8,128)S(1)} %fusion.8), channel_id=1, replica_groups=mesh['row'=8,'col'=4] {'row'}, dimensions={0} | all-to-all | bytes 2621440 | tf_op jit(solution)/shard_map/all_to_all | solution.py:104
  41.6 0.0 copy-done.3
  41.6 1.3 %convolution_bitcast_fusion = f32[1,256,1280]{2,1,0:T(8,128)S(1)} fusion(f32[256,256]{1,0:T(8,128)S(1)} %copy-done.3, f32[256,1280]{1,0:T(8,128)S(1)} %bitcast.146), kind=kOutput, calls=%fused_computation | convolution fusion | flops 1006632960 | bytes 2883584 | tf_op jit(solution)/shard_map/...jc,ji->...ic/dot_general | solution.py:57
  42.9 2.4 %copy.17 = f32[1,256,1280]{2,0,1:T(1,128)} copy(f32[1,256,1280]{2,1,0:T(8,128)S(1)} %convolution_bitcast_fusion) | data formatting | bytes 2621440 | tf_op jit(solution)/shard_map/...jc,ji->...ic/transpose | solution.py:57
  45.3 4.3 %all-to-all-start.1 = ((f32[1,256,1280]{2,0,1:T(1,128)}), f32[1,256,1280]{2,0,1:T(1,128)}, u32[]{:S(2)}, u32[]{:S(2)}) async-start(f32[1,256,1280]{2,0,1:T(1,128)} %copy.17), calls=%async_computation.1 | async-start | bytes 2621440 | tf_op jit(solution)/shard_map/all_to_all | solution.py:108
  49.5 0.1 multiply_bitcast_fusion
  49.8 0.1 fusion.7
  50.0 0.0 copy-start.4
  50.1 0.8 copy-done.4
  50.9 3.5 %convolution_bitcast_fusion.1 = f32[5,1,32,16,384]{4,3,2,0,1:T(8,128)S(1)} fusion(f32[5,32,16,128]{3,2,1,0:T(8,128)S(1)} %bitcast_dynamic-update-slice_fusion, f32[128,384,1,1]{1,0,3,2:T(8,128)S(1)} %copy-done.4), kind=kOutput, calls=%fused_computation.1 | convolution fusion | flops 1509949440 | bytes 5439488 | tf_op jit(solution)/shard_map/...bj,jk->...bk/dot_general | solution.py:42
  54.4 0.1 fusion.18
  54.5 0.2 fusion.17
  54.8 0.4 fusion
  55.1 0.2 reshape.138
  55.3 24.9 %all-to-all-done.1 = f32[1,256,1280]{2,0,1:T(1,128)} async-done(((f32[1,256,1280]{2,0,1:T(1,128)}), f32[1,256,1280]{2,0,1:T(1,128)}, u32[]{:S(2)}, u32[]{:S(2)}) %all-to-all-start.1) | async-done | bytes 1310752 | tf_op jit(solution)/shard_map/all_to_all | solution.py:108
  80.3 3.1 %copy.29 = f32[1,8,32,1280]{3,1,2,0:T(8,128)} copy(f32[1,8,32,1280]{3,0,2,1:T(1,128)} %bitcast.24) | data formatting | bytes 2621440 | tf_op jit(solution)/shard_map/all_to_all | solution.py:108
  83.4 1.5 %reshape.141 = f32[1,32,5,2048]{3,2,1,0:T(8,128)S(1)} reshape(f32[1,32,8,1280]{3,2,1,0:T(8,128)} %bitcast.147) | data formatting | bytes 2621440 | tf_op jit(solution)/shard_map/reshape | solution.py:109
  84.9 2.0 %fusion.1 = f32[5,1,32,2048]{3,2,1,0:T(8,128)} fusion(f32[5,1,32,2048]{3,2,1,0:T(8,128)S(1)} %reshape.138, f32[1,32,5,2048]{3,2,1,0:T(8,128)S(1)} %reshape.141), kind=kLoop, calls=%fused_computation.5 | loop fusion | flops 655360 | bytes 3932160 | tf_op jit(solution)/shard_map/neg | solution.py:110
  (21 shorter events, 0.6 us)
Async XLA Ops:
  0.0 2.5 %copy-start = (f32[3,1,32,2048]{3,2,1,0:T(8,128)S(1)}, f32[3,1,32,2048]{3,2,1,0:T(8,128)}, u32[]{:S(2)}) copy-start(f32[3,1,32,2048]{3,2,1,0:T(8,128)} %param.6) | copy-start | bytes 2359300
  1.0 1.5 %copy-start.1 = (f32[1,32,2048]{2,1,0:T(8,128)S(1)}, f32[1,32,2048]{2,1,0:T(8,128)}, u32[]{:S(2)}) copy-start(f32[1,32,2048]{2,1,0:T(8,128)} %param.7) | copy-start | bytes 786436
  1.1 1.5 %copy-start.2 = (f32[1,32,2048]{2,1,0:T(8,128)S(1)}, f32[1,32,2048]{2,1,0:T(8,128)}, u32[]{:S(2)}) copy-start(f32[1,32,2048]{2,1,0:T(8,128)} %param.5) | copy-start | bytes 786436
  3.0 38.6 %copy-start.3 = (f32[256,256]{1,0:T(8,128)S(1)}, f32[256,256]{1,0:T(8,128)}, u32[]{:S(2)}) copy-start(f32[256,256]{1,0:T(8,128)} %constant.11.clone) | copy-start | bytes 786436
  45.3 35.0 %all-to-all-start.1 = ((f32[1,256,1280]{2,0,1:T(1,128)}), f32[1,256,1280]{2,0,1:T(1,128)}, u32[]{:S(2)}, u32[]{:S(2)}) async-start(f32[1,256,1280]{2,0,1:T(1,128)} %copy.17), calls=%async_computation.1 | async-start | bytes 2621440 | tf_op jit(solution)/shard_map/all_to_all | solution.py:108
  50.0 0.9 %copy-start.4 = (f32[128,384,1,1]{1,0,3,2:T(8,128)S(1)}, f32[128,384,1,1]{1,0,3,2:T(8,128)}, u32[]{:S(2)}) copy-start(f32[128,384,1,1]{1,0,3,2:T(8,128)} %constant.15) | copy-start | bytes 589828
